TPU v7x, 32 devices: a whole 2x2x4 slice. The times are simulated.
32 devices in a mesh: pipe: 4 (over z), et: 8 (over y, x, core).
Axes of the slice: x: 2, y: 2, z: 4, core: 2. Of those that a mesh axis runs over, the one named last changes fastest.
Arguments:
- tokens: bfloat16 [4, 1024, 4096], P('pipe', 'et'), may hold values from -6 to 6
- gate_vals: bfloat16 [4, 1024, 2], P('pipe', 'et'), may hold values from 0.099609375 to 1
- expert_ids: int32 [4, 1024, 2], P('pipe', 'et'), may hold values from 0 to 7, as said below
- grad_out: bfloat16 [4, 1024, 4096], P('pipe', 'et'), may hold values from -6 to 6
- w_gate: bfloat16 [4, 2, 4096, 7168], P('pipe', None, None, 'et'), may hold values from -0.09375 to 0.09375
- w_up: bfloat16 [4, 2, 4096, 7168], P('pipe', None, None, 'et'), may hold values from -0.09375 to 0.09375
- w_down: bfloat16 [4, 2, 7168, 4096], P('pipe', None, 'et'), may hold values from -0.0625 to 0.0625
Outputs:
- moe_out: bfloat16 [4, 1024, 4096], P('pipe', 'et')
- prior_grads: bfloat16 [4, 1024, 4096], P('pipe', 'et')
Inputs may be any that keep to these rules, and one draw needn't show every extreme that they name: `expert_ids`: each row names 2 different experts. The rows of one device of one section name each of experts 0 to 1 at most 16 times, and for each of these experts there is a section in which every device's rows name it exactly 16 times.
All inputs are finite; a program needn't handle non-finite values.
Results may differ from a plain program's by a relative error of at most 0.012.
Values may be sent and summed in bfloat16 or wider, within the bound.
No kernel may reach another device: no remote copies, remote signals or barrier semaphores. Data moves between devices by JAX's collectives and lax.ppermute only.
A program may use at most 192 MiB of HBM per device.

v0:
```python
import jax
import jax.numpy as jnp
from jax import lax
from jax.sharding import PartitionSpec as P

E_WIN = 2
MOST = 16
TAIL = 128


def shifted(value, axis, steps):
    count = lax.axis_size(axis)
    first, last = (max(0, -steps), min(count, count - steps))
    return lax.ppermute(value, axis, [(source, source + steps) for source in range(first, last)])


def silu_parts(pre_gate):
    sigma = jax.nn.sigmoid(pre_gate)
    return (pre_gate * sigma, sigma * (1.0 + pre_gate * (1.0 - sigma)))


def local_slots(local_routes, local_gates):
    slot_ids = jnp.arange(MOST, dtype=jnp.int32)[:, None]
    selects, weights = ([], [])
    for expert in range(E_WIN):
        matches = local_routes == expert
        routed = jnp.any(matches, axis=1)
        gate_val = jnp.sum(jnp.where(matches, local_gates.astype(jnp.float32), 0.0), axis=1)
        positions = jnp.cumsum(routed.astype(jnp.int32), dtype=jnp.int32) - 1
        select = routed[None, :] & (positions[None, :] == slot_ids)
        selects.append(select)
        weights.append(jnp.sum(jnp.where(select, gate_val[None, :], 0.0), axis=1))
    return (jnp.concatenate(selects, axis=0), jnp.concatenate(weights))


def pick_rows(select, rows):
    return jnp.dot(select.astype(rows.dtype), rows, preferred_element_type=jnp.float32).astype(
        rows.dtype
    )


def halve_over_et(parts):
    n = lax.axis_size("et")
    me = lax.axis_index("et")
    held = parts
    bit = 1
    while 2 * bit < n:
        halves = held.reshape((held.shape[0] // 2, 2) + held.shape[1:])
        side = me // bit % 2
        keep = jnp.take(halves, side, axis=1)
        give = jnp.take(halves, 1 - side, axis=1)
        got = lax.ppermute(give, "et", [(i, i ^ bit) for i in range(n)])
        held = (keep.astype(jnp.float32) + got.astype(jnp.float32)).astype(jnp.bfloat16)
        bit *= 2
    side = me // bit % 2
    return (jnp.take(held, side, axis=0), jnp.take(held, 1 - side, axis=0), bit)


def reduce_to_owner(parts):
    n = lax.axis_size("et")
    keep, give, bit = halve_over_et(parts)
    got = lax.ppermute(give, "et", [(i, i ^ bit) for i in range(n)])
    return keep.astype(jnp.float32) + got.astype(jnp.float32)


def reduce_to_previous(parts):
    n = lax.axis_size("et")
    stages = lax.axis_size("pipe")
    keep, give, bit = halve_over_et(parts)
    to_same = [(stage * n + i, (stage - 1) * n + i) for stage in range(1, stages) for i in range(n)]
    to_other = [
        (stage * n + i, (stage - 1) * n + (i ^ bit)) for stage in range(1, stages) for i in range(n)
    ]
    first = lax.ppermute(keep, ("pipe", "et"), to_same)
    second = lax.ppermute(give, ("pipe", "et"), to_other)
    return first.astype(jnp.float32) + second.astype(jnp.float32)


def unpack(slot_sums, select):
    return lax.dot_general(
        select.astype(jnp.float32),
        slot_sums,
        (((0,), (0,)), ((), ())),
        precision=lax.Precision.HIGHEST,
        preferred_element_type=jnp.float32,
    ).astype(jnp.bfloat16)


def per_device(tokens, gate_vals, expert_ids, grad_out, w_gate, w_up, w_down):
    local_rows = tokens[0]
    local_grads = grad_out[0]
    gate_mats = w_gate[0]
    up_mats = w_up[0]
    down_mats = w_down[0]
    n = lax.axis_size("et")
    width = local_rows.shape[1]
    select, weights = local_slots(expert_ids[0], gate_vals[0])
    next_routes = shifted(expert_ids[0], "pipe", -1)
    next_select = local_slots(next_routes, gate_vals[0])[0]
    weight_cols = jnp.broadcast_to(weights.astype(jnp.bfloat16)[:, None], (E_WIN * MOST, TAIL))
    packed = jnp.concatenate(
        [pick_rows(select, local_rows), pick_rows(select, local_grads), weight_cols], axis=1
    )
    gathered = lax.all_gather(packed, "et", axis=0, tiled=True).reshape(
        n, E_WIN, MOST, 2 * width + TAIL
    )
    outs = []
    stored = []
    for expert in range(E_WIN):
        rows = gathered[:, expert, :, :width].reshape(n * MOST, width)
        gate_w = gathered[:, expert, :, 2 * width].reshape(n * MOST, 1).astype(jnp.float32)
        pre_gate = jnp.dot(rows, gate_mats[expert], preferred_element_type=jnp.float32)
        pre_up = jnp.dot(rows, up_mats[expert], preferred_element_type=jnp.float32)
        activated, slopes = silu_parts(pre_gate)
        hidden = (activated * pre_up).astype(jnp.bfloat16)
        out_e = gate_w * jnp.dot(hidden, down_mats[expert], preferred_element_type=jnp.float32)
        outs.append(out_e.astype(jnp.bfloat16).reshape(n, MOST, width))
        stored.append((gate_w, pre_up, activated, slopes))
    out_parts = jnp.stack(outs, axis=1).reshape(n, E_WIN * MOST, width)
    out_sums = reduce_to_owner(out_parts)
    grad_outs = []
    for expert in range(E_WIN):
        gate_w, pre_up, activated, slopes = stored[expert]
        grad_rows = gathered[:, expert, :, width : 2 * width].reshape(n * MOST, width)
        d_hidden = gate_w * lax.dot_general(
            grad_rows,
            down_mats[expert],
            (((1,), (1,)), ((), ())),
            preferred_element_type=jnp.float32,
        )
        d_gate = (d_hidden * pre_up * slopes).astype(jnp.bfloat16)
        d_up = (d_hidden * activated).astype(jnp.bfloat16)
        grad_e = lax.dot_general(
            d_gate, gate_mats[expert], (((1,), (1,)), ((), ())), preferred_element_type=jnp.float32
        ) + lax.dot_general(
            d_up, up_mats[expert], (((1,), (1,)), ((), ())), preferred_element_type=jnp.float32
        )
        grad_outs.append(grad_e.astype(jnp.bfloat16).reshape(n, MOST, width))
    grad_parts = jnp.stack(grad_outs, axis=1).reshape(n, E_WIN * MOST, width)
    out_sums, grad_parts = lax.optimization_barrier((out_sums, grad_parts))
    received = unpack(reduce_to_previous(grad_parts), next_select)
    out_share = unpack(out_sums, select)
    return (out_share[None], received[None])


def solution(mesh):
    placed = (
        P("pipe", "et", None),
        P("pipe", "et", None),
        P("pipe", "et", None),
        P("pipe", "et", None),
        P("pipe", None, None, "et"),
        P("pipe", None, None, "et"),
        P("pipe", None, "et", None),
    )
    return jax.shard_map(
        per_device,
        mesh=mesh,
        in_specs=placed,
        out_specs=(P("pipe", "et", None), P("pipe", "et", None)),
        check_vma=False,
    )
```

profile of v0, /device:TPU:0, one launch (start us, length us, event | category | flops | bytes accessed | tf_op | source)
XLA Modules:
  0.0 167.1 jit_solution(3968941739426077450)
XLA Ops:
  9.8 1.5 convolution_convert_fusion.3
  12.6 39.7 %all-gather.2.cloned.1.call-done = bf16[256,8320]{1,0:T(8,128)(2,1)} async-done(((bf16[32,8320]{1,0:T(8,128)(2,1)}), bf16[256,8320]{1,0:T(8,128)(2,1)}) %all-gather.2.cloned.1.call-update) | async-done | bytes 4259856 | tf_op jit(solution)/shard_map/all_gather | solution.py:104
  53.3 2.9 %fusion.103 = (bf16[8,1,16,4096]{3,2,1,0:T(8,128)(2,1)S(1)}, bf16[8,1,16,4096]{3,2,1,0:T(8,128)(2,1)S(1)}, bf16[8,1,16,4096]{3,2,1,0:T(8,128)(2,1)S(1)}, bf16[8,1,16,4096]{3,2,1,0:T(8,128)(2,1)S(1)}) fusion(bf16[8,2,16,8320]{3,2,1,0:T(8,128)(2,1)} %bitcast.175), kind=kLoop, calls=%fused_computation.132 | loop fusion | bytes 8388608 | tf_op jit(solution)/shard_map/slice | solution.py:124
  56.2 5.2 %fusion.6 = f32[128,896]{1,0:T(8,128)S(1)} fusion(bf16[128,4096]{1,0:T(8,128)(2,1)S(1)} %bitcast.188, bf16[1,2,4096,896]{3,2,1,0:T(8,128)(2,1)} %param.18), kind=kOutput, calls=%fused_computation.6 | convolution fusion | flops 939524096 | bytes 8847360 | tf_op jit(solution)/shard_map/dot_general | solution.py:113
  61.4 2.1 %fusion.10 = f32[128,896]{1,0:T(8,128)} fusion(bf16[128,4096]{1,0:T(8,128)(2,1)S(1)} %bitcast.189, bf16[1,2,4096,896]{3,2,1,0:T(8,128)(2,1)S(1)} %copy-done.3), kind=kOutput, calls=%fused_computation.10 | convolution fusion | flops 939524096 | bytes 8847360 | tf_op jit(solution)/shard_map/dot_general | solution.py:112
  68.5 4.7 %fusion.48 = bf16[128,4096]{1,0:T(8,128)(2,1)S(1)} fusion(bf16[1,2,896,4096]{3,2,1,0:T(8,128)(2,1)} %param.19, f32[128]{0:T(128)S(1)} %reshape.401, f32[128,896]{1,0:T(8,128)S(1)} %fusion.6, f32[128,896]{1,0:T(8,128)} %fusion.10), kind=kOutput, calls=%fused_computation.40 | convolution fusion | flops 941260800 | bytes 9306624 | tf_op jit(solution)/shard_map/dot_general | solution.py:116
  73.2 4.5 %fusion.54 = bf16[128,4096]{1,0:T(8,128)(2,1)S(1)} fusion(bf16[1,2,896,4096]{3,2,1,0:T(8,128)(2,1)} %param.19, f32[128]{0:T(128)S(1)} %reshape.400, f32[128,896]{1,0:T(8,128)S(1)} %fusion.18, f32[128,896]{1,0:T(8,128)S(1)} %fusion.22), kind=kOutput, calls=%fused_computation.42 | convolution fusion | flops 941260800 | bytes 9306624 | tf_op jit(solution)/shard_map/dot_general | solution.py:116
  78.4 2.4 %fusion.65 = f32[128,896]{1,0:T(8,128)S(1)} fusion(bf16[128,4096]{1,0:T(8,128)(2,1)S(1)} %bitcast.185, bf16[1,2,896,4096]{3,2,1,0:T(8,128)(2,1)S(1)} %bitcast.192, f32[128]{0:T(128)S(1)} %reshape.401), kind=kOutput, calls=%fused_computation.55 | convolution fusion | flops 939638784 | bytes 8847872 | tf_op jit(solution)/shard_map/dot_general | solution.py:125
  80.9 5.7 %fusion.4 = f32[128,4096]{1,0:T(8,128)S(1)} fusion(bf16[1,2,4096,896]{3,2,1,0:T(8,128)(2,1)} %param.18, f32[128,896]{1,0:T(8,128)S(1)} %fusion.65, f32[128,896]{1,0:T(8,128)S(1)} %copy-done.4), kind=kOutput, calls=%fused_computation.4 | convolution fusion | flops 940212224 | bytes 10354688 | tf_op jit(solution)/shard_map/dot_general | solution.py:135
  86.6 2.4 %fusion.62 = f32[128,896]{1,0:T(8,128)S(1)} fusion(bf16[128,4096]{1,0:T(8,128)(2,1)S(1)} %bitcast.184, bf16[1,2,896,4096]{3,2,1,0:T(8,128)(2,1)S(1)} %bitcast.192, f32[128]{0:T(128)S(1)} %reshape.400), kind=kOutput, calls=%fused_computation.54 | convolution fusion | flops 939638784 | bytes 8847872 | tf_op jit(solution)/shard_map/dot_general | solution.py:125
  89.0 5.5 %fusion.16 = f32[128,4096]{1,0:T(8,128)S(1)} fusion(bf16[1,2,4096,896]{3,2,1,0:T(8,128)(2,1)} %param.18, f32[128,896]{1,0:T(8,128)S(1)} %fusion.62, f32[128,896]{1,0:T(8,128)S(1)} %fusion.22), kind=kOutput, calls=%fused_computation.16 | convolution fusion | flops 940212224 | bytes 10354688 | tf_op jit(solution)/shard_map/dot_general | solution.py:135
  94.5 5.6 %fusion.51 = bf16[128,4096]{1,0:T(8,128)(2,1)S(1)} fusion(f32[128,4096]{1,0:T(8,128)S(1)} %fusion.4, bf16[1,2,4096,896]{3,2,1,0:T(8,128)(2,1)} %param.17, f32[128,896]{1,0:T(8,128)S(1)} %copy-done.4, f32[128,896]{1,0:T(8,128)S(1)} %fusion.65, f32[128,896]{1,0:T(8,128)S(1)} %fusion.6), kind=kOutput, calls=%fused_computation.41 | convolution fusion | flops 941719552 | bytes 11862016 | tf_op jit(solution)/shard_map/dot_general | solution.py:133
  100.5 1.5 collective-permute-start.1
  102.1 5.6 %fusion.57 = bf16[128,4096]{1,0:T(8,128)(2,1)S(1)} fusion(f32[128,4096]{1,0:T(8,128)S(1)} %fusion.16, bf16[1,2,4096,896]{3,2,1,0:T(8,128)(2,1)} %param.17, f32[128,896]{1,0:T(8,128)S(1)} %fusion.22, f32[128,896]{1,0:T(8,128)S(1)} %fusion.62, f32[128,896]{1,0:T(8,128)S(1)} %fusion.18), kind=kOutput, calls=%fused_computation.43 | convolution fusion | flops 941719552 | bytes 11862016 | tf_op jit(solution)/shard_map/dot_general | solution.py:133
  107.7 7.0 %collective-permute-done.1 = bf16[2,32,4096]{2,1,0:T(8,128)(2,1)S(1)} collective-permute-done((bf16[2,32,4096]{2,1,0:T(8,128)(2,1)S(1)}, bf16[2,32,4096]{2,1,0:T(8,128)(2,1)S(1)}, u32[]{:S(2)}, u32[]{:S(2)}) %collective-permute-start.1) | collective-permute-done | bytes 524320 | tf_op jit(solution)/shard_map/ppermute | solution.py:52
  114.9 1.4 collective-permute-start.2
  116.5 6.1 %collective-permute-done.2 = bf16[32,4096]{1,0:T(8,128)(2,1)S(1)} collective-permute-done((bf16[32,4096]{1,0:T(8,128)(2,1)S(1)}, bf16[32,4096]{1,0:T(8,128)(2,1)S(1)}, u32[]{:S(2)}, u32[]{:S(2)}) %collective-permute-start.2) | collective-permute-done | bytes 262176 | tf_op jit(solution)/shard_map/ppermute | solution.py:62
  124.2 4.2 %collective-permute-done.3 = s32[128,2]{0,1:T(2,128)S(1)} collective-permute-done((s32[128,2]{0,1:T(2,128)S(1)}, s32[128,2]{0,1:T(2,128)S(1)}, u32[]{:S(2)}, u32[]{:S(2)}) %collective-permute-start.3) | collective-permute-done | bytes 1056 | tf_op jit(solution)/shard_map/ppermute | solution.py:14
  128.8 1.5 collective-permute-start.5
  131.1 11.0 %collective-permute-done.5 = bf16[2,32,4096]{2,1,0:T(8,128)(2,1)} collective-permute-done((bf16[2,32,4096]{2,1,0:T(8,128)(2,1)S(1)}, bf16[2,32,4096]{2,1,0:T(8,128)(2,1)}, u32[]{:S(2)}, u32[]{:S(2)}) %collective-permute-start.5) | collective-permute-done | bytes 524320 | tf_op jit(solution)/shard_map/ppermute | solution.py:52
  146.0 2.0 %fusion.60 = bf16[1,128,4096]{2,1,0:T(8,128)(2,1)} fusion(f32[32,4096]{1,0:T(8,128)S(1)} %convert_add_fusion, pred[16,128]{1,0:T(8,128)(4,1)S(1)} %get-tuple-element.59, pred[16,128]{1,0:T(8,128)(4,1)S(1)} %get-tuple-element.58), kind=kOutput, calls=%fused_computation.46 | convolution fusion | flops 201854976 | bytes 1576960 | tf_op jit(solution)/shard_map/dot_general | solution.py:80
  148.0 7.4 %collective-permute-done.7 = bf16[32,4096]{1,0:T(8,128)(2,1)S(1)} collective-permute-done((bf16[32,4096]{1,0:T(8,128)(2,1)S(1)}, bf16[32,4096]{1,0:T(8,128)(2,1)S(1)}, u32[]{:S(2)}, u32[]{:S(2)}) %collective-permute-start.7) | collective-permute-done | bytes 262176 | tf_op jit(solution)/shard_map/ppermute | solution.py:75
  155.4 2.9 %collective-permute-done.6 = bf16[32,4096]{1,0:T(8,128)(2,1)S(1)} collective-permute-done((bf16[32,4096]{1,0:T(8,128)(2,1)S(1)}, bf16[32,4096]{1,0:T(8,128)(2,1)S(1)}, u32[]{:S(2)}, u32[]{:S(2)}) %collective-permute-start.6) | collective-permute-done | bytes 262176 | tf_op jit(solution)/shard_map/ppermute | solution.py:74
  158.3 2.0 %fusion.61 = bf16[1,128,4096]{2,1,0:T(8,128)(2,1)} fusion(bf16[32,4096]{1,0:T(8,128)(2,1)S(1)} %collective-permute-done.7, bf16[32,4096]{1,0:T(8,128)(2,1)S(1)} %collective-permute-done.6, pred[16,128]{1,0:T(8,128)(4,1)S(1)} %get-tuple-element.61, pred[16,128]{1,0:T(8,128)(4,1)S(1)} %get-tuple-element.60), kind=kOutput, calls=%fused_computation.47 | convolution fusion | flops 202248192 | bytes 1576960 | tf_op jit(solution)/shard_map/dot_general | solution.py:80
  (83 shorter events, 17.7 us)
Async XLA Ops:
  7.2 2.4 %copy-start = (bf16[1,128,4096]{2,1,0:T(8,128)(2,1)S(1)}, bf16[1,128,4096]{2,1,0:T(8,128)(2,1)}, u32[]{:S(2)}) copy-start(bf16[1,128,4096]{2,1,0:T(8,128)(2,1)} %param.16) | copy-start | bytes 3145732
  7.2 45.1 %all-gather.2.cloned.1.call-start = ((), (), s32[]{:S(2)}) async-start(), calls=%async_computation | async-start | bytes 4792320 | tf_op jit(solution)/shard_map/all_gather | solution.py:104
  52.3 9.1 %copy-start.3 = (bf16[1,2,4096,896]{3,2,1,0:T(8,128)(2,1)S(1)}, bf16[1,2,4096,896]{3,2,1,0:T(8,128)(2,1)}, u32[]{:S(2)}) copy-start(bf16[1,2,4096,896]{3,2,1,0:T(8,128)(2,1)} %param.17) | copy-start | bytes 44040196
  53.2 10.3 %slice-start.4 = ((s8[14680064]{0:T(1024)(128)(4,1)}), s8[4194304]{0:T(1024)(128)(4,1)S(1)}, s32[]{:S(2)}) async-start(s8[14680064]{0:T(1024)(128)(4,1)} %bitcast.193), calls=%async_computation.5 | async-start | bytes 8388608
  53.2 10.3 %slice-start.5 = ((s8[14680064]{0:T(1024)(128)(4,1)}), s8[4194304]{0:T(1024)(128)(4,1)S(1)}, s32[]{:S(2)}) async-start(s8[14680064]{0:T(1024)(128)(4,1)} %bitcast.193), calls=%async_computation.6 | async-start | bytes 8388608
  56.2 8.7 %slice-start.6 = ((s8[14680064]{0:T(1024)(128)(4,1)}), s8[4194304]{0:T(1024)(128)(4,1)S(1)}, s32[]{:S(2)}) async-start(s8[14680064]{0:T(1024)(128)(4,1)} %bitcast.193), calls=%async_computation.7 | async-start | bytes 8388608
  61.4 4.0 %slice-start.7 = ((s8[14680064]{0:T(1024)(128)(4,1)}), s8[2097152]{0:T(1024)(128)(4,1)S(1)}, s32[]{:S(2)}) async-start(s8[14680064]{0:T(1024)(128)(4,1)} %bitcast.193), calls=%async_computation.8 | async-start | bytes 4194304
  68.5 9.9 %slice-start = ((s8[14680064]{0:T(1024)(128)(4,1)}), s8[4194304]{0:T(1024)(128)(4,1)S(1)}, s32[]{:S(2)}) async-start(s8[14680064]{0:T(1024)(128)(4,1)} %bitcast.191), calls=%async_computation.1 | async-start | bytes 8388608
  68.5 9.9 %slice-start.1 = ((s8[14680064]{0:T(1024)(128)(4,1)}), s8[4194304]{0:T(1024)(128)(4,1)S(1)}, s32[]{:S(2)}) async-start(s8[14680064]{0:T(1024)(128)(4,1)} %bitcast.191), calls=%async_computation.2 | async-start | bytes 8388608
  73.2 5.2 %slice-start.2 = ((s8[14680064]{0:T(1024)(128)(4,1)}), s8[4194304]{0:T(1024)(128)(4,1)S(1)}, s32[]{:S(2)}) async-start(s8[14680064]{0:T(1024)(128)(4,1)} %bitcast.191), calls=%async_computation.3 | async-start | bytes 8388608
  73.2 5.2 %slice-start.3 = ((s8[14680064]{0:T(1024)(128)(4,1)}), s8[2097152]{0:T(1024)(128)(4,1)S(1)}, s32[]{:S(2)}) async-start(s8[14680064]{0:T(1024)(128)(4,1)} %bitcast.191), calls=%async_computation.4 | async-start | bytes 4194304
  77.9 2.9 %copy-start.4 = (f32[128,896]{1,0:T(8,128)S(1)}, f32[128,896]{1,0:T(8,128)}, u32[]{:S(2)}) copy-start(f32[128,896]{1,0:T(8,128)} %fusion.10) | copy-start | bytes 1376260
  78.1 22.0 %collective-permute-start = (bf16[4,32,4096]{2,1,0:T(8,128)(2,1)S(1)}, bf16[4,32,4096]{2,1,0:T(8,128)(2,1)S(1)}, u32[]{:S(2)}, u32[]{:S(2)}) collective-permute-start(bf16[4,32,4096]{2,1,0:T(8,128)(2,1)S(1)} %select_bitcast_fusion.1), channel_id=1, source_target_pairs={{0,1},{1,0},{2,3},{3,2},{4,5},{5,4},{6,7},{7,6},{8,9},{9,8},{10,11... | collective-permute-start | bytes 3145736 | tf_op jit(solution)/shard_map/ppermute | solution.py:52
  100.5 14.1 %collective-permute-start.1 = (bf16[2,32,4096]{2,1,0:T(8,128)(2,1)S(1)}, bf16[2,32,4096]{2,1,0:T(8,128)(2,1)S(1)}, u32[]{:S(2)}, u32[]{:S(2)}) collective-permute-start(bf16[2,32,4096]{2,1,0:T(8,128)(2,1)S(1)} %select_bitcast_fusion.3), channel_id=1, source_target_pairs={{0,2},{1,3},{2,0},{3,1},{4,6},{5,7},{6,4},{7,5},{8,10},{9,11},{10,... | collective-permute-start | bytes 1572872 | tf_op jit(solution)/shard_map/ppermute | solution.py:52
  107.7 15.2 %copy-start.2 = (s32[1,128,2]{1,2,0:T(2,128)S(1)}, s32[1,128,2]{1,2,0:T(2,128)}, u32[]{:S(2)}) copy-start(s32[1,128,2]{1,2,0:T(2,128)} %param.15) | copy-start | bytes 3076
  114.9 7.7 %collective-permute-start.2 = (bf16[32,4096]{1,0:T(8,128)(2,1)S(1)}, bf16[32,4096]{1,0:T(8,128)(2,1)S(1)}, u32[]{:S(2)}, u32[]{:S(2)}) collective-permute-start(bf16[32,4096]{1,0:T(8,128)(2,1)S(1)} %select_bitcast_fusion.6), channel_id=1, source_target_pairs={{0,4},{1,5},{2,6},{3,7},{4,0},{5,1},{6,2},{7,3},{8,12},{9,13},{10,... | collective-permute-start | bytes 786440 | tf_op jit(solution)/shard_map/ppermute | solution.py:62
  116.3 44.0 %copy-start.1 = (bf16[1,128,4096]{2,1,0:T(8,128)(2,1)S(1)}, bf16[1,128,4096]{2,1,0:T(8,128)(2,1)}, u32[]{:S(2)}) copy-start(bf16[1,128,4096]{2,1,0:T(8,128)(2,1)} %param.16) | copy-start | bytes 3145732
  122.8 5.6 %collective-permute-start.4 = (bf16[4,32,4096]{2,1,0:T(8,128)(2,1)S(1)}, bf16[4,32,4096]{2,1,0:T(8,128)(2,1)S(1)}, u32[]{:S(2)}, u32[]{:S(2)}) collective-permute-start(bf16[4,32,4096]{2,1,0:T(8,128)(2,1)S(1)} %select_bitcast_fusion), channel_id=1, source_target_pairs={{0,1},{1,0},{2,3},{3,2},{4,5},{5,4},{6,7},{7,6},{8,9},{9,8},{10,11... | collective-permute-start | bytes 3145736 | tf_op jit(solution)/shard_map/ppermute | solution.py:52
  122.9 5.5 %collective-permute-start.3 = (s32[128,2]{0,1:T(2,128)S(1)}, s32[128,2]{0,1:T(2,128)S(1)}, u32[]{:S(2)}, u32[]{:S(2)}) collective-permute-start(s32[128,2]{0,1:T(2,128)S(1)} %bitcast.190), channel_id=1, source_target_pairs={{8,0},{16,8},{24,16},{9,1},{17,9},{25,17},{10,2},{18,10},{26,18},{... | collective-permute-start | bytes 3080 | tf_op jit(solution)/shard_map/ppermute | solution.py:14
  128.8 13.3 %collective-permute-start.5 = (bf16[2,32,4096]{2,1,0:T(8,128)(2,1)S(1)}, bf16[2,32,4096]{2,1,0:T(8,128)(2,1)}, u32[]{:S(2)}, u32[]{:S(2)}) collective-permute-start(bf16[2,32,4096]{2,1,0:T(8,128)(2,1)S(1)} %select_bitcast_fusion.2), channel_id=1, source_target_pairs={{0,2},{1,3},{2,0},{3,1},{4,6},{5,7},{6,4},{7,5},{8,10},{9,11},{10,... | collective-permute-start | bytes 1572872 | tf_op jit(solution)/shard_map/ppermute | solution.py:52
  143.4 12.0 %collective-permute-start.7 = (bf16[32,4096]{1,0:T(8,128)(2,1)S(1)}, bf16[32,4096]{1,0:T(8,128)(2,1)S(1)}, u32[]{:S(2)}, u32[]{:S(2)}) collective-permute-start(bf16[32,4096]{1,0:T(8,128)(2,1)S(1)} %get-tuple-element.55), channel_id=1, source_target_pairs={{8,4},{9,5},{10,6},{11,7},{12,0},{13,1},{14,2},{15,3},{16,12},{17,... | collective-permute-start | bytes 786440 | tf_op jit(solution)/shard_map/ppermute | solution.py:75
  144.7 13.6 %collective-permute-start.6 = (bf16[32,4096]{1,0:T(8,128)(2,1)S(1)}, bf16[32,4096]{1,0:T(8,128)(2,1)S(1)}, u32[]{:S(2)}, u32[]{:S(2)}) collective-permute-start(bf16[32,4096]{1,0:T(8,128)(2,1)S(1)} %get-tuple-element.54), channel_id=1, source_target_pairs={{8,0},{9,1},{10,2},{11,3},{12,4},{13,5},{14,6},{15,7},{16,8},{17,9... | collective-permute-start | bytes 786440 | tf_op jit(solution)/shard_map/ppermute | solution.py:74
Sparse Core Ops, SparseCore 0:
  12.6 39.6 all-gather.1
where the time goes:
time: 168 us; the launch traced here: 167 us
  waiting for transfers between devices  78.3 us (47%)
  matrix products  52 us (31%)
  between operations  14.6 us (9%)
  starting transfers between devices  8.75 us (5%)
  local copies, waits for them, and re-layouts  6.88 us (4%)
  other arithmetic  6.58 us (4%)
    all_gather x1, waiting for transfers between devices, per_device(): lax.all_gather(packed, 'et', axis=0, tiled=True)  39.7 us
    ppermute x4, waiting for transfers between devices, halve_over_et(): got = lax.ppermute(give, 'et', [(i, i ^ bit) for i in range(n)])  18 us
    dot_general x2, matrix products, per_device(): lax.dot_general(d_up, up_mats[expert], (((1,), (1,)), ((), ())), preferre...  11.2 us
    dot_general x2, matrix products, per_device(): lax.dot_general(d_gate, gate_mats[expert], (((1,), (1,)), ((), ())), pref...  11.2 us
    dot_general x2, matrix products, per_device(): jnp.dot(hidden, down_mats[expert], preferred_element_type=jnp.float32)  9.21 us
    ppermute x1, waiting for transfers between devices, reduce_to_previous(): second = lax.ppermute(give, ('pipe', 'et'), to_other)  7.42 us
    dot_general x2, matrix products, per_device(): pre_up = jnp.dot(rows, up_mats[expert], preferred_element_type=jnp.float32)  6.48 us
    ppermute x1, waiting for transfers between devices, reduce_to_owner(): got = lax.ppermute(give, 'et', [(i, i ^ bit) for i in range(n)])  6.13 us
  transfers between devices with their start and end apart: 9, of which 7 were waited for; matrix products, arithmetic and copies ran while one was open for 18% of the time, Pallas kernels for 0%

commit v1 on v0

--- a/solution.py
+++ b/solution.py
@@ -6,6 +6,16 @@
 E_WIN = 2
 MOST = 16
 TAIL = 128
+
+
+def ring_gather(x, axis, dim):
+    ways, here, step = (lax.axis_size(axis), lax.axis_index(axis), x.shape[dim])
+    shape = [n * ways if d == dim else n for d, n in enumerate(x.shape)]
+    full = lax.dynamic_update_slice_in_dim(jnp.zeros(shape, x.dtype), x, here * step, axis=dim)
+    for far in range(1, ways):
+        x = lax.ppermute(x, axis, [(d, (d + 1) % ways) for d in range(ways)])
+        full = lax.dynamic_update_slice_in_dim(full, x, (here - far) % ways * step, axis=dim)
+    return full
 
 
 def shifted(value, axis, steps):
@@ -101,9 +111,7 @@
     packed = jnp.concatenate(
         [pick_rows(select, local_rows), pick_rows(select, local_grads), weight_cols], axis=1
     )
-    gathered = lax.all_gather(packed, "et", axis=0, tiled=True).reshape(
-        n, E_WIN, MOST, 2 * width + TAIL
-    )
+    gathered = ring_gather(packed, "et", 0).reshape(n, E_WIN, MOST, 2 * width + TAIL)
     outs = []
     stored = []
     for expert in range(E_WIN):

time: 168 us -> 184 us (1.095)
  waiting for transfers between devices: 78.3 us -> 103 us
  between operations: 14.6 us -> 1.11 us
  local copies, waits for them, and re-layouts: 6.88 us -> 12.4 us
    ppermute x0 -> x7, waiting for transfers between devices: none -> 62.3 us  [ring_gather(): x = lax.ppermute(x, axis, [(d, (d + 1) % ways) for d in range(ways)])]
    all_gather x1 -> x0, waiting for transfers between devices: 39.7 us -> none  [per_device(): lax.all_gather(packed, 'et', axis=0, tiled=True)]
    dynamic_update_slice x0 -> x7, local copies, waits for them, and re-layouts: none -> 5.86 us  [ring_gather(): lax.dynamic_update_slice_in_dim(full, x, (here - far) % ways * step, axis...]
    dot_general x2, matrix products: 6.48 us -> 2.53 us  [per_device(): pre_up = jnp.dot(rows, up_mats[expert], preferred_element_type=jnp.float32)]
    dot_general x2, matrix products: 3.33 us -> 6.96 us  [per_device(): jnp.dot(rows, gate_mats[expert], preferred_element_type=jnp.float32)]
    ppermute x4, starting transfers between devices: 3.46 us -> 1.12 us  [halve_over_et(): got = lax.ppermute(give, 'et', [(i, i ^ bit) for i in range(n)])]
    ppermute x4, waiting for transfers between devices: 18 us -> 20.3 us  [halve_over_et(): got = lax.ppermute(give, 'et', [(i, i ^ bit) for i in range(n)])]
    broadcast_in_dim x0 -> x1, local copies, waits for them, and re-layouts: none -> 2.25 us  [ring_gather(): jnp.zeros(shape, x.dtype)]
  transfers between devices with their start and end apart: 9 -> 15, of which waited for: 7 -> 13; matrix products, arithmetic and copies ran while one was open for 18% -> 19% of each run, Pallas kernels for 0% -> 0%
where the time goes in v1:
time: 184 us
  waiting for transfers between devices  103 us (56%)
  matrix products  51.8 us (28%)
  local copies, waits for them, and re-layouts  12.4 us (7%)
  starting transfers between devices  7.81 us (4%)
  other arithmetic  7.5 us (4%)
    ppermute x7, waiting for transfers between devices, ring_gather(): x = lax.ppermute(x, axis, [(d, (d + 1) % ways) for d in range(ways)])  62.3 us
    ppermute x4, waiting for transfers between devices, halve_over_et(): got = lax.ppermute(give, 'et', [(i, i ^ bit) for i in range(n)])  20.3 us
    dot_general x2, matrix products, per_device(): lax.dot_general(d_gate, gate_mats[expert], (((1,), (1,)), ((), ())), pref...  11.2 us
    dot_general x2, matrix products, per_device(): lax.dot_general(d_up, up_mats[expert], (((1,), (1,)), ((), ())), preferre...  11.1 us
    dot_general x2, matrix products, per_device(): jnp.dot(hidden, down_mats[expert], preferred_element_type=jnp.float32)  9.21 us
    ppermute x1, waiting for transfers between devices, reduce_to_previous(): second = lax.ppermute(give, ('pipe', 'et'), to_other)  7.42 us
    dot_general x2, matrix products, per_device(): jnp.dot(rows, gate_mats[expert], preferred_element_type=jnp.float32)  6.96 us
    dynamic_update_slice x7, local copies, waits for them, and re-layouts, ring_gather(): lax.dynamic_update_slice_in_dim(full, x, (here - far) % ways * step, axis...  5.86 us
  transfers between devices with their start and end apart: 15, of which 13 were waited for; matrix products, arithmetic and copies ran while one was open for 19% of the time, Pallas kernels for 0%

profile of v1, /device:TPU:0, one launch (start us, length us, event | category | flops | bytes accessed | tf_op | source)
XLA Modules:
  0.0 183.9 jit_solution(8991123186404990363)
XLA Ops:
  8.6 9.8 %collective-permute-done = bf16[32,8320]{1,0:T(8,128)(2,1)S(1)} collective-permute-done((bf16[32,8320]{1,0:T(8,128)(2,1)S(1)}, bf16[32,8320]{1,0:T(8,128)(2,1)S(1)}, u32[]{:S(2)}, u32[]{:S(2)}) %collective-permute-start) | collective-permute-done | bytes 532512 | tf_op jit(solution)/shard_map/ppermute | solution.py:16
  19.3 8.8 %collective-permute-done.1 = bf16[32,8320]{1,0:T(8,128)(2,1)S(1)} collective-permute-done((bf16[32,8320]{1,0:T(8,128)(2,1)S(1)}, bf16[32,8320]{1,0:T(8,128)(2,1)S(1)}, u32[]{:S(2)}, u32[]{:S(2)}) %collective-permute-start.1) | collective-permute-done | bytes 532512 | tf_op jit(solution)/shard_map/ppermute | solution.py:16
  28.9 8.8 %collective-permute-done.2 = bf16[32,8320]{1,0:T(8,128)(2,1)S(1)} collective-permute-done((bf16[32,8320]{1,0:T(8,128)(2,1)S(1)}, bf16[32,8320]{1,0:T(8,128)(2,1)S(1)}, u32[]{:S(2)}, u32[]{:S(2)}) %collective-permute-start.2) | collective-permute-done | bytes 532512 | tf_op jit(solution)/shard_map/ppermute | solution.py:16
  38.5 8.8 %collective-permute-done.3 = bf16[32,8320]{1,0:T(8,128)(2,1)S(1)} collective-permute-done((bf16[32,8320]{1,0:T(8,128)(2,1)S(1)}, bf16[32,8320]{1,0:T(8,128)(2,1)S(1)}, u32[]{:S(2)}, u32[]{:S(2)}) %collective-permute-start.3) | collective-permute-done | bytes 532512 | tf_op jit(solution)/shard_map/ppermute | solution.py:16
  48.0 8.8 %collective-permute-done.4 = bf16[32,8320]{1,0:T(8,128)(2,1)S(1)} collective-permute-done((bf16[32,8320]{1,0:T(8,128)(2,1)S(1)}, bf16[32,8320]{1,0:T(8,128)(2,1)S(1)}, u32[]{:S(2)}, u32[]{:S(2)}) %collective-permute-start.4) | collective-permute-done | bytes 532512 | tf_op jit(solution)/shard_map/ppermute | solution.py:16
  57.7 8.7 %collective-permute-done.5 = bf16[32,8320]{1,0:T(8,128)(2,1)S(1)} collective-permute-done((bf16[32,8320]{1,0:T(8,128)(2,1)S(1)}, bf16[32,8320]{1,0:T(8,128)(2,1)S(1)}, u32[]{:S(2)}, u32[]{:S(2)}) %collective-permute-start.5) | collective-permute-done | bytes 532512 | tf_op jit(solution)/shard_map/ppermute | solution.py:16
  67.3 8.7 %collective-permute-done.6 = bf16[32,8320]{1,0:T(8,128)(2,1)S(1)} collective-permute-done((bf16[32,8320]{1,0:T(8,128)(2,1)S(1)}, bf16[32,8320]{1,0:T(8,128)(2,1)S(1)}, u32[]{:S(2)}, u32[]{:S(2)}) %collective-permute-start.6) | collective-permute-done | bytes 532512 | tf_op jit(solution)/shard_map/ppermute | solution.py:16
  77.7 2.6 %fusion.103 = (bf16[8,1,16,4096]{3,2,1,0:T(8,128)(2,1)S(1)}, bf16[8,1,16,4096]{3,2,1,0:T(8,128)(2,1)S(1)}, bf16[8,1,16,4096]{3,2,1,0:T(8,128)(2,1)S(1)}, bf16[8,1,16,4096]{3,2,1,0:T(8,128)(2,1)S(1)}) fusion(bf16[8,2,16,8320]{3,2,1,0:T(8,128)(2,1)} %bitcast.7), kind=kLoop, calls=%fused_computation.142 | loop fusion | bytes 8388608 | tf_op jit(solution)/shard_map/slice | solution.py:132
  81.6 5.7 %fusion.10 = f32[128,896]{1,0:T(8,128)} fusion(bf16[128,4096]{1,0:T(8,128)(2,1)S(1)} %bitcast.179, bf16[1,2,4096,896]{3,2,1,0:T(8,128)(2,1)} %param.17), kind=kOutput, calls=%fused_computation.10 | convolution fusion | flops 939524096 | bytes 8847360 | tf_op jit(solution)/shard_map/dot_general | solution.py:120
  90.9 4.7 %fusion.48 = bf16[128,4096]{1,0:T(8,128)(2,1)S(1)} fusion(bf16[1,2,896,4096]{3,2,1,0:T(8,128)(2,1)} %param.19, f32[128]{0:T(128)S(1)} %reshape.401, f32[128,896]{1,0:T(8,128)S(1)} %fusion.6, f32[128,896]{1,0:T(8,128)} %fusion.10), kind=kOutput, calls=%fused_computation.40 | convolution fusion | flops 941260800 | bytes 9306624 | tf_op jit(solution)/shard_map/dot_general | solution.py:124
  95.6 4.5 %fusion.54 = bf16[128,4096]{1,0:T(8,128)(2,1)S(1)} fusion(bf16[1,2,896,4096]{3,2,1,0:T(8,128)(2,1)} %param.19, f32[128]{0:T(128)S(1)} %reshape.400, f32[128,896]{1,0:T(8,128)S(1)} %fusion.18, f32[128,896]{1,0:T(8,128)S(1)} %fusion.22), kind=kOutput, calls=%fused_computation.42 | convolution fusion | flops 941260800 | bytes 9306624 | tf_op jit(solution)/shard_map/dot_general | solution.py:124
  100.7 2.5 %fusion.65 = f32[128,896]{1,0:T(8,128)S(1)} fusion(bf16[128,4096]{1,0:T(8,128)(2,1)S(1)} %bitcast.175, bf16[1,2,896,4096]{3,2,1,0:T(8,128)(2,1)S(1)} %bitcast.182, f32[128]{0:T(128)S(1)} %reshape.401), kind=kOutput, calls=%fused_computation.55 | convolution fusion | flops 939638784 | bytes 8847872 | tf_op jit(solution)/shard_map/dot_general | solution.py:133
  103.2 5.5 %fusion.4 = f32[128,4096]{1,0:T(8,128)S(1)} fusion(bf16[1,2,4096,896]{3,2,1,0:T(8,128)(2,1)} %param.18, f32[128,896]{1,0:T(8,128)S(1)} %fusion.65, f32[128,896]{1,0:T(8,128)S(1)} %copy-done.4), kind=kOutput, calls=%fused_computation.4 | convolution fusion | flops 940212224 | bytes 10354688 | tf_op jit(solution)/shard_map/dot_general | solution.py:143
  108.8 2.7 %fusion.62 = f32[128,896]{1,0:T(8,128)S(1)} fusion(bf16[128,4096]{1,0:T(8,128)(2,1)S(1)} %bitcast.174, bf16[1,2,896,4096]{3,2,1,0:T(8,128)(2,1)S(1)} %bitcast.182, f32[128]{0:T(128)S(1)} %reshape.400), kind=kOutput, calls=%fused_computation.54 | convolution fusion | flops 939638784 | bytes 8847872 | tf_op jit(solution)/shard_map/dot_general | solution.py:133
  111.4 5.5 %fusion.16 = f32[128,4096]{1,0:T(8,128)S(1)} fusion(bf16[1,2,4096,896]{3,2,1,0:T(8,128)(2,1)} %param.18, f32[128,896]{1,0:T(8,128)S(1)} %fusion.62, f32[128,896]{1,0:T(8,128)S(1)} %fusion.22), kind=kOutput, calls=%fused_computation.16 | convolution fusion | flops 940212224 | bytes 10354688 | tf_op jit(solution)/shard_map/dot_general | solution.py:143
  117.0 5.6 %fusion.51 = bf16[128,4096]{1,0:T(8,128)(2,1)S(1)} fusion(f32[128,4096]{1,0:T(8,128)S(1)} %fusion.4, bf16[1,2,4096,896]{3,2,1,0:T(8,128)(2,1)} %param.17, f32[128,896]{1,0:T(8,128)S(1)} %copy-done.4, f32[128,896]{1,0:T(8,128)S(1)} %fusion.65, f32[128,896]{1,0:T(8,128)S(1)} %fusion.6), kind=kOutput, calls=%fused_computation.41 | convolution fusion | flops 941719552 | bytes 11862016 | tf_op jit(solution)/shard_map/dot_general | solution.py:141
  123.3 5.6 %fusion.57 = bf16[128,4096]{1,0:T(8,128)(2,1)S(1)} fusion(f32[128,4096]{1,0:T(8,128)S(1)} %fusion.16, bf16[1,2,4096,896]{3,2,1,0:T(8,128)(2,1)} %param.17, f32[128,896]{1,0:T(8,128)S(1)} %fusion.22, f32[128,896]{1,0:T(8,128)S(1)} %fusion.62, f32[128,896]{1,0:T(8,128)S(1)} %fusion.18), kind=kOutput, calls=%fused_computation.43 | convolution fusion | flops 941719552 | bytes 11862016 | tf_op jit(solution)/shard_map/dot_general | solution.py:141
  128.9 8.3 %collective-permute-done.8 = bf16[2,32,4096]{2,1,0:T(8,128)(2,1)S(1)} collective-permute-done((bf16[2,32,4096]{2,1,0:T(8,128)(2,1)S(1)}, bf16[2,32,4096]{2,1,0:T(8,128)(2,1)S(1)}, u32[]{:S(2)}, u32[]{:S(2)}) %collective-permute-start.8) | collective-permute-done | bytes 524320 | tf_op jit(solution)/shard_map/ppermute | solution.py:62
  137.5 2.3 %collective-permute-start.9 = (bf16[32,4096]{1,0:T(8,128)(2,1)S(1)}, bf16[32,4096]{1,0:T(8,128)(2,1)S(1)}, u32[]{:S(2)}, u32[]{:S(2)}) collective-permute-start(bf16[32,4096]{1,0:T(8,128)(2,1)S(1)} %select_bitcast_fusion.6), channel_id=1, source_target_pairs={{0,4},{1,5},{2,6},{3,7},{4,0},{5,1},{6,2},{7,3},{8,12},{9,13},{10,... | collective-permute-start | bytes 786440 | tf_op jit(solution)/shard_map/ppermute | solution.py:72
  140.0 5.8 %collective-permute-done.9 = bf16[32,4096]{1,0:T(8,128)(2,1)S(1)} collective-permute-done((bf16[32,4096]{1,0:T(8,128)(2,1)S(1)}, bf16[32,4096]{1,0:T(8,128)(2,1)S(1)}, u32[]{:S(2)}, u32[]{:S(2)}) %collective-permute-start.9) | collective-permute-done | bytes 262176 | tf_op jit(solution)/shard_map/ppermute | solution.py:72
  147.4 4.2 %collective-permute-done.10 = s32[128,2]{0,1:T(2,128)S(1)} collective-permute-done((s32[128,2]{0,1:T(2,128)S(1)}, s32[128,2]{0,1:T(2,128)S(1)}, u32[]{:S(2)}, u32[]{:S(2)}) %collective-permute-start.10) | collective-permute-done | bytes 1056 | tf_op jit(solution)/shard_map/ppermute | solution.py:24
  153.4 12.0 %collective-permute-done.12 = bf16[2,32,4096]{2,1,0:T(8,128)(2,1)} collective-permute-done((bf16[2,32,4096]{2,1,0:T(8,128)(2,1)S(1)}, bf16[2,32,4096]{2,1,0:T(8,128)(2,1)}, u32[]{:S(2)}, u32[]{:S(2)}) %collective-permute-start.12) | collective-permute-done | bytes 524320 | tf_op jit(solution)/shard_map/ppermute | solution.py:62
  171.3 7.4 %collective-permute-done.14 = bf16[32,4096]{1,0:T(8,128)(2,1)S(1)} collective-permute-done((bf16[32,4096]{1,0:T(8,128)(2,1)S(1)}, bf16[32,4096]{1,0:T(8,128)(2,1)S(1)}, u32[]{:S(2)}, u32[]{:S(2)}) %collective-permute-start.14) | collective-permute-done | bytes 262176 | tf_op jit(solution)/shard_map/ppermute | solution.py:85
  178.7 3.2 %collective-permute-done.13 = bf16[32,4096]{1,0:T(8,128)(2,1)S(1)} collective-permute-done((bf16[32,4096]{1,0:T(8,128)(2,1)S(1)}, bf16[32,4096]{1,0:T(8,128)(2,1)S(1)}, u32[]{:S(2)}, u32[]{:S(2)}) %collective-permute-start.13) | collective-permute-done | bytes 262176 | tf_op jit(solution)/shard_map/ppermute | solution.py:84
  (100 shorter events, 32.4 us)
Async XLA Ops:
  8.1 10.3 %collective-permute-start = (bf16[32,8320]{1,0:T(8,128)(2,1)S(1)}, bf16[32,8320]{1,0:T(8,128)(2,1)S(1)}, u32[]{:S(2)}, u32[]{:S(2)}) collective-permute-start(bf16[32,8320]{1,0:T(8,128)(2,1)S(1)} %get-tuple-element.54), channel_id=1, source_target_pairs={{0,1},{1,2},{2,3},{3,4},{4,5},{5,6},{6,7},{7,0},{8,9},{9,10},{10,1... | collective-permute-start | bytes 1597448 | tf_op jit(solution)/shard_map/ppermute | solution.py:16
  18.4 9.6 %collective-permute-start.1 = (bf16[32,8320]{1,0:T(8,128)(2,1)S(1)}, bf16[32,8320]{1,0:T(8,128)(2,1)S(1)}, u32[]{:S(2)}, u32[]{:S(2)}) collective-permute-start(bf16[32,8320]{1,0:T(8,128)(2,1)S(1)} %collective-permute-done), channel_id=1, source_target_pairs={{0,1},{1,2},{2,3},{3,4},{4,5},{5,6},{6,7},{7,0},{8,9},{9,10},{10,1... | collective-permute-start | bytes 1597448 | tf_op jit(solution)/shard_map/ppermute | solution.py:16
  28.0 9.6 %collective-permute-start.2 = (bf16[32,8320]{1,0:T(8,128)(2,1)S(1)}, bf16[32,8320]{1,0:T(8,128)(2,1)S(1)}, u32[]{:S(2)}, u32[]{:S(2)}) collective-permute-start(bf16[32,8320]{1,0:T(8,128)(2,1)S(1)} %collective-permute-done.1), channel_id=1, source_target_pairs={{0,1},{1,2},{2,3},{3,4},{4,5},{5,6},{6,7},{7,0},{8,9},{9,10},{10,1... | collective-permute-start | bytes 1597448 | tf_op jit(solution)/shard_map/ppermute | solution.py:16
  28.0 52.3 %copy-start.3 = (bf16[1,2,4096,896]{3,2,1,0:T(8,128)(2,1)S(1)}, bf16[1,2,4096,896]{3,2,1,0:T(8,128)(2,1)}, u32[]{:S(2)}) copy-start(bf16[1,2,4096,896]{3,2,1,0:T(8,128)(2,1)} %param.18) | copy-start | bytes 44040196
  37.6 9.6 %collective-permute-start.3 = (bf16[32,8320]{1,0:T(8,128)(2,1)S(1)}, bf16[32,8320]{1,0:T(8,128)(2,1)S(1)}, u32[]{:S(2)}, u32[]{:S(2)}) collective-permute-start(bf16[32,8320]{1,0:T(8,128)(2,1)S(1)} %collective-permute-done.2), channel_id=1, source_target_pairs={{0,1},{1,2},{2,3},{3,4},{4,5},{5,6},{6,7},{7,0},{8,9},{9,10},{10,1... | collective-permute-start | bytes 1597448 | tf_op jit(solution)/shard_map/ppermute | solution.py:16
  47.2 9.6 %collective-permute-start.4 = (bf16[32,8320]{1,0:T(8,128)(2,1)S(1)}, bf16[32,8320]{1,0:T(8,128)(2,1)S(1)}, u32[]{:S(2)}, u32[]{:S(2)}) collective-permute-start(bf16[32,8320]{1,0:T(8,128)(2,1)S(1)} %collective-permute-done.3), channel_id=1, source_target_pairs={{0,1},{1,2},{2,3},{3,4},{4,5},{5,6},{6,7},{7,0},{8,9},{9,10},{10,1... | collective-permute-start | bytes 1597448 | tf_op jit(solution)/shard_map/ppermute | solution.py:16
  56.8 9.6 %collective-permute-start.5 = (bf16[32,8320]{1,0:T(8,128)(2,1)S(1)}, bf16[32,8320]{1,0:T(8,128)(2,1)S(1)}, u32[]{:S(2)}, u32[]{:S(2)}) collective-permute-start(bf16[32,8320]{1,0:T(8,128)(2,1)S(1)} %collective-permute-done.4), channel_id=1, source_target_pairs={{0,1},{1,2},{2,3},{3,4},{4,5},{5,6},{6,7},{7,0},{8,9},{9,10},{10,1... | collective-permute-start | bytes 1597448 | tf_op jit(solution)/shard_map/ppermute | solution.py:16
  66.4 9.6 %collective-permute-start.6 = (bf16[32,8320]{1,0:T(8,128)(2,1)S(1)}, bf16[32,8320]{1,0:T(8,128)(2,1)S(1)}, u32[]{:S(2)}, u32[]{:S(2)}) collective-permute-start(bf16[32,8320]{1,0:T(8,128)(2,1)S(1)} %collective-permute-done.5), channel_id=1, source_target_pairs={{0,1},{1,2},{2,3},{3,4},{4,5},{5,6},{6,7},{7,0},{8,9},{9,10},{10,1... | collective-permute-start | bytes 1597448 | tf_op jit(solution)/shard_map/ppermute | solution.py:16
  80.3 8.3 %slice-start.4 = ((s8[14680064]{0:T(1024)(128)(4,1)}), s8[4194304]{0:T(1024)(128)(4,1)S(1)}, s32[]{:S(2)}) async-start(s8[14680064]{0:T(1024)(128)(4,1)} %bitcast.183), calls=%async_computation.4 | async-start | bytes 8388608
  80.3 8.3 %slice-start.5 = ((s8[14680064]{0:T(1024)(128)(4,1)}), s8[2097152]{0:T(1024)(128)(4,1)S(1)}, s32[]{:S(2)}) async-start(s8[14680064]{0:T(1024)(128)(4,1)} %bitcast.183), calls=%async_computation.5 | async-start | bytes 4194304
  81.6 7.0 %slice-start.6 = ((s8[14680064]{0:T(1024)(128)(4,1)}), s8[4194304]{0:T(1024)(128)(4,1)S(1)}, s32[]{:S(2)}) async-start(s8[14680064]{0:T(1024)(128)(4,1)} %bitcast.183), calls=%async_computation.6 | async-start | bytes 8388608
  90.9 9.7 %slice-start = ((s8[14680064]{0:T(1024)(128)(4,1)}), s8[4194304]{0:T(1024)(128)(4,1)S(1)}, s32[]{:S(2)}) async-start(s8[14680064]{0:T(1024)(128)(4,1)} %bitcast.181), calls=%async_computation | async-start | bytes 8388608
  90.9 9.7 %slice-start.1 = ((s8[14680064]{0:T(1024)(128)(4,1)}), s8[4194304]{0:T(1024)(128)(4,1)S(1)}, s32[]{:S(2)}) async-start(s8[14680064]{0:T(1024)(128)(4,1)} %bitcast.181), calls=%async_computation.1 | async-start | bytes 8388608
  95.6 5.1 %slice-start.3 = ((s8[14680064]{0:T(1024)(128)(4,1)}), s8[2097152]{0:T(1024)(128)(4,1)S(1)}, s32[]{:S(2)}) async-start(s8[14680064]{0:T(1024)(128)(4,1)} %bitcast.181), calls=%async_computation.3 | async-start | bytes 4194304
  100.5 22.1 %collective-permute-start.7 = (bf16[4,32,4096]{2,1,0:T(8,128)(2,1)S(1)}, bf16[4,32,4096]{2,1,0:T(8,128)(2,1)S(1)}, u32[]{:S(2)}, u32[]{:S(2)}) collective-permute-start(bf16[4,32,4096]{2,1,0:T(8,128)(2,1)S(1)} %select_bitcast_fusion.1), channel_id=1, source_target_pairs={{0,1},{1,0},{2,3},{3,2},{4,5},{5,4},{6,7},{7,6},{8,9},{9,8},{10,11... | collective-permute-start | bytes 3145736 | tf_op jit(solution)/shard_map/ppermute | solution.py:62
  123.0 14.3 %collective-permute-start.8 = (bf16[2,32,4096]{2,1,0:T(8,128)(2,1)S(1)}, bf16[2,32,4096]{2,1,0:T(8,128)(2,1)S(1)}, u32[]{:S(2)}, u32[]{:S(2)}) collective-permute-start(bf16[2,32,4096]{2,1,0:T(8,128)(2,1)S(1)} %select_bitcast_fusion.3), channel_id=1, source_target_pairs={{0,2},{1,3},{2,0},{3,1},{4,6},{5,7},{6,4},{7,5},{8,10},{9,11},{10,... | collective-permute-start | bytes 1572872 | tf_op jit(solution)/shard_map/ppermute | solution.py:62
  137.4 8.7 %copy-start.2 = (s32[1,128,2]{1,2,0:T(2,128)S(1)}, s32[1,128,2]{1,2,0:T(2,128)}, u32[]{:S(2)}) copy-start(s32[1,128,2]{1,2,0:T(2,128)} %param.15) | copy-start | bytes 3076
  137.5 8.4 %collective-permute-start.9 = (bf16[32,4096]{1,0:T(8,128)(2,1)S(1)}, bf16[32,4096]{1,0:T(8,128)(2,1)S(1)}, u32[]{:S(2)}, u32[]{:S(2)}) collective-permute-start(bf16[32,4096]{1,0:T(8,128)(2,1)S(1)} %select_bitcast_fusion.6), channel_id=1, source_target_pairs={{0,4},{1,5},{2,6},{3,7},{4,0},{5,1},{6,2},{7,3},{8,12},{9,13},{10,... | collective-permute-start | bytes 786440 | tf_op jit(solution)/shard_map/ppermute | solution.py:72
  146.0 5.6 %collective-permute-start.11 = (bf16[4,32,4096]{2,1,0:T(8,128)(2,1)S(1)}, bf16[4,32,4096]{2,1,0:T(8,128)(2,1)S(1)}, u32[]{:S(2)}, u32[]{:S(2)}) collective-permute-start(bf16[4,32,4096]{2,1,0:T(8,128)(2,1)S(1)} %select_bitcast_fusion), channel_id=1, source_target_pairs={{0,1},{1,0},{2,3},{3,2},{4,5},{5,4},{6,7},{7,6},{8,9},{9,8},{10,11... | collective-permute-start | bytes 3145736 | tf_op jit(solution)/shard_map/ppermute | solution.py:62
  146.1 5.5 %collective-permute-start.10 = (s32[128,2]{0,1:T(2,128)S(1)}, s32[128,2]{0,1:T(2,128)S(1)}, u32[]{:S(2)}, u32[]{:S(2)}) collective-permute-start(s32[128,2]{0,1:T(2,128)S(1)} %bitcast.180), channel_id=1, source_target_pairs={{8,0},{16,8},{24,16},{9,1},{17,9},{25,17},{10,2},{18,10},{26,18},{... | collective-permute-start | bytes 3080 | tf_op jit(solution)/shard_map/ppermute | solution.py:24
  151.6 32.3 %copy-start.1 = (bf16[1,128,4096]{2,1,0:T(8,128)(2,1)S(1)}, bf16[1,128,4096]{2,1,0:T(8,128)(2,1)}, u32[]{:S(2)}) copy-start(bf16[1,128,4096]{2,1,0:T(8,128)(2,1)} %param.16) | copy-start | bytes 3145732
  152.0 13.4 %collective-permute-start.12 = (bf16[2,32,4096]{2,1,0:T(8,128)(2,1)S(1)}, bf16[2,32,4096]{2,1,0:T(8,128)(2,1)}, u32[]{:S(2)}, u32[]{:S(2)}) collective-permute-start(bf16[2,32,4096]{2,1,0:T(8,128)(2,1)S(1)} %select_bitcast_fusion.2), channel_id=1, source_target_pairs={{0,2},{1,3},{2,0},{3,1},{4,6},{5,7},{6,4},{7,5},{8,10},{9,11},{10,... | collective-permute-start | bytes 1572872 | tf_op jit(solution)/shard_map/ppermute | solution.py:62
  166.7 12.0 %collective-permute-start.14 = (bf16[32,4096]{1,0:T(8,128)(2,1)S(1)}, bf16[32,4096]{1,0:T(8,128)(2,1)S(1)}, u32[]{:S(2)}, u32[]{:S(2)}) collective-permute-start(bf16[32,4096]{1,0:T(8,128)(2,1)S(1)} %get-tuple-element.57), channel_id=1, source_target_pairs={{8,4},{9,5},{10,6},{11,7},{12,0},{13,1},{14,2},{15,3},{16,12},{17,... | collective-permute-start | bytes 786440 | tf_op jit(solution)/shard_map/ppermute | solution.py:85
  168.0 13.9 %collective-permute-start.13 = (bf16[32,4096]{1,0:T(8,128)(2,1)S(1)}, bf16[32,4096]{1,0:T(8,128)(2,1)S(1)}, u32[]{:S(2)}, u32[]{:S(2)}) collective-permute-start(bf16[32,4096]{1,0:T(8,128)(2,1)S(1)} %get-tuple-element.56), channel_id=1, source_target_pairs={{8,0},{9,1},{10,2},{11,3},{12,4},{13,5},{14,6},{15,7},{16,8},{17,9... | collective-permute-start | bytes 786440 | tf_op jit(solution)/shard_map/ppermute | solution.py:84
  (4 other events, 12.0 us)
